TPU v7x, 32 devices: a whole 2x2x4 slice. The times are simulated.
32 devices in a mesh: group: 2 (over y), ctx: 4 (over z), head: 2 (over x), sub: 2 (over core).
Axes of the slice: x: 2, y: 2, z: 4, core: 2. Of those that a mesh axis runs over, the one named last changes fastest.
Arguments:
- queries: bfloat16 [4, 4096, 128], P(('head', 'sub'), ('group', 'ctx')), parts along dimension 1, may hold values from -18 to 18
- keys: bfloat16 [4, 4096, 128], P(('head', 'sub'), ('group', 'ctx')), parts along dimension 1, may hold values from -6 to 6
- values: bfloat16 [4, 4096, 128], P(('head', 'sub'), ('group', 'ctx')), parts along dimension 1, may hold values from -6 to 6
- stick_offset: float32 [4], P(('head', 'sub')), may hold values from -14 to -7
Outputs:
- attended: bfloat16 [4, 4096, 128], P(('head', 'sub'), ('group', 'ctx')), parts along dimension 1
There are 2 independent parts, one for each index of `group`. A program takes and returns all parts, laid end to end along the dimension named above; an argument that names none is the same for every part. Nothing has to cross between parts.
All inputs are finite; a program needn't handle non-finite values.
Results may differ from a plain program's by a relative error of at most 0.0049.
Values may be sent and summed in bfloat16 or wider, within the bound.
No kernel may reach another device: no remote copies, remote signals or barrier semaphores. Data moves between devices by JAX's collectives and lax.ppermute only.
A program may use at most 64 MiB of HBM per device.

v0:
```python
import functools
import math

import jax
import numpy as np
import jax.numpy as jnp
from jax import lax
from jax.experimental import pallas as pl
from jax.experimental.pallas import tpu as pltpu
from jax.sharding import PartitionSpec as P


ROW_TILE = 256


def pair_kernel(scalar_ref, q_ref, kv_ref, upper_ref, *refs, diag, scale, last):
    if diag:
        summed_ref, spent_ref = refs
    else:
        in_summed_ref, in_spent_ref, summed_ref = refs[:3]
        spent_ref = None if last else refs[3]
    tile, _ = q_ref.shape
    keys = kv_ref.shape[0] // 2
    score = (
        lax.dot_general(
            q_ref[...],
            kv_ref[:keys, :],
            (((1,), (1,)), ((), ())),
            preferred_element_type=jnp.float32,
        )
        * scale
        + scalar_ref[0]
    )
    soft = jnp.log1p(jnp.exp(-jnp.abs(score)))
    spent = jnp.maximum(score, 0.0) + soft
    logsig = jnp.minimum(score, 0.0) - soft
    if diag:
        row = pl.program_id(0) * tile + lax.broadcasted_iota(jnp.int32, (tile, keys), 0)
        col = lax.broadcasted_iota(jnp.int32, (tile, keys), 1)
        live = col < row
        spent = jnp.where(live, spent, 0.0)
    upper = upper_ref[...]
    high = spent.astype(jnp.bfloat16)
    low = (spent - high.astype(jnp.float32)).astype(jnp.bfloat16)
    later = jnp.dot(high, upper, preferred_element_type=jnp.float32) + jnp.dot(
        low, upper, preferred_element_type=jnp.float32
    )
    weight = jnp.exp(logsig - later)
    if diag:
        weight = jnp.where(live, weight, 0.0)
    part = jnp.dot(weight.astype(jnp.bfloat16), kv_ref[keys:, :], preferred_element_type=jnp.float32)
    tot = later[:, 0:1] + spent[:, 0:1]
    if diag:
        summed_ref[...] = part
        spent_ref[...] = tot
        return
    use = scalar_ref[1] > 0.0
    before = in_spent_ref[...]
    summed = jnp.where(use, in_summed_ref[...] + jnp.exp(-before) * part, in_summed_ref[...])
    summed_ref[...] = summed.astype(summed_ref.dtype)
    if not last:
        spent_ref[...] = jnp.where(use, before + tot, before)


def pair_terms(q, kv, upper, scalars, carried=None, last=False):
    rows, width = q.shape
    keys = kv.shape[0] // 2
    tile = min(ROW_TILE, rows)
    diag = carried is None
    kernel = functools.partial(
        pair_kernel, diag=diag, scale=1.0 / math.sqrt(width), last=last
    )
    flops = 2 * rows * keys * (2 * width + 2 * keys)
    rows_spec = pl.BlockSpec((tile, width), lambda r: (r, 0))
    col_spec = pl.BlockSpec((tile, 1), lambda r: (r, 0))
    in_specs = [
        pl.BlockSpec(memory_space=pltpu.SMEM),
        rows_spec,
        pl.BlockSpec((2 * keys, width), lambda r: (0, 0)),
        pl.BlockSpec((keys, keys), lambda r: (0, 0)),
    ]
    args = [scalars, q, kv, upper]
    if not diag:
        in_specs += [rows_spec, col_spec]
        args += list(carried)
    out_specs = [rows_spec]
    out_shape = [jax.ShapeDtypeStruct((rows, width), jnp.bfloat16 if last else jnp.float32)]
    if not last:
        out_specs.append(col_spec)
        out_shape.append(jax.ShapeDtypeStruct((rows, 1), jnp.float32))
    return pl.pallas_call(
        kernel,
        grid=(rows // tile,),
        in_specs=in_specs,
        out_specs=out_specs,
        out_shape=out_shape,
        cost_estimate=pl.CostEstimate(
            flops=flops, transcendentals=3 * rows * keys, bytes_accessed=rows * width * 16
        ),
    )(*args)


def one_head(q_own, k_own, v_own, offset):
    count = lax.axis_size("ctx")
    place = lax.axis_index("ctx")
    route = [(i, (i + 1) % count) for i in range(count)]
    keys = k_own.shape[0]
    upper = jnp.asarray(np.triu(np.ones((keys, keys), np.float32), 1).T, jnp.bfloat16)
    kv = jnp.concatenate([k_own, v_own], axis=0)
    steps = jnp.arange(count, dtype=jnp.int32)
    table = jnp.stack(
        [jnp.broadcast_to(offset, (count,)), jnp.where(place >= steps, 1.0, 0.0)], axis=1
    ).astype(jnp.float32)
    carried = pair_terms(q_own, kv, upper, table[0])
    for step in range(1, count):
        kv = lax.ppermute(kv, "ctx", route)
        carried = pair_terms(
            q_own, kv, upper, table[step], carried, last=step == count - 1
        )
    if count == 1:
        return carried[0].astype(jnp.bfloat16)
    return carried[0]


def on_device(queries, keys, values, stick_offset):
    results = []
    for h in range(queries.shape[0]):
        results.append(one_head(queries[h], keys[h], values[h], stick_offset[h]))
    return jnp.stack(results, axis=0)


def solution(mesh):
    placed = (
        P(("head", "sub"), ("group", "ctx"), None),
        P(("head", "sub"), ("group", "ctx"), None),
        P(("head", "sub"), ("group", "ctx"), None),
        P(("head", "sub")),
    )
    return jax.shard_map(
        on_device,
        mesh=mesh,
        in_specs=placed,
        out_specs=P(("head", "sub"), ("group", "ctx"), None),
        check_vma=False,
    )
```

profile of v0, /device:TPU:0, one launch (start us, length us, event | category | flops | bytes accessed | tf_op | source)
XLA Modules:
  0.0 39.0 jit_solution(5638564770640085169)
XLA Ops:
  0.0 1.0 %pad_maximum_fusion.kv_ref = bf16[1024,128]{1,0:T(8,128)(2,1)S(1)} fusion(bf16[512,128]{1,0:T(8,128)(2,1)} %bitcast.14, bf16[512,128]{1,0:T(8,128)(2,1)} %bitcast.15), kind=kLoop, calls=%fused_computation | loop fusion | flops 524288 | bytes 524288 | tf_op jit(solution)/shard_map/concatenate | solution.py:109
  1.0 0.0 copy-start
  1.0 3.1 %collective-permute-start = (bf16[1024,128]{1,0:T(8,128)(2,1)S(1)}, bf16[1024,128]{1,0:T(8,128)(2,1)S(1)}, u32[]{:S(2)}, u32[]{:S(2)}) collective-permute-start(bf16[1024,128]{1,0:T(8,128)(2,1)S(1)} %pad_maximum_fusion.kv_ref), channel_id=1, source_target_pairs={{0,4},{4,8},{8,12},{12,0},{1,5},{5,9},{9,13},{13,1},{2,6},{6,10},{... | collective-permute-start | bytes 786440 | tf_op jit(solution)/shard_map/ppermute | solution.py:116
  4.1 8.3 %collective-permute-done.kv_ref = bf16[1024,128]{1,0:T(8,128)(2,1)S(1)} collective-permute-done((bf16[1024,128]{1,0:T(8,128)(2,1)S(1)}, bf16[1024,128]{1,0:T(8,128)(2,1)S(1)}, u32[]{:S(2)}, u32[]{:S(2)}) %collective-permute-start) | collective-permute-done | bytes 262176 | tf_op jit(solution)/shard_map/ppermute | solution.py:116
  12.4 0.0 copy-start.2
  12.4 0.0 collective-permute-start.1
  13.1 8.6 %collective-permute-done.1.kv_ref = bf16[1024,128]{1,0:T(8,128)(2,1)S(1)} collective-permute-done((bf16[1024,128]{1,0:T(8,128)(2,1)S(1)}, bf16[1024,128]{1,0:T(8,128)(2,1)S(1)}, u32[]{:S(2)}, u32[]{:S(2)}) %collective-permute-start.1) | collective-permute-done | bytes 262176 | tf_op jit(solution)/shard_map/ppermute | solution.py:116
  21.7 0.0 copy-start.1
  21.7 0.0 collective-permute-start.2
  21.7 0.7 %fusion.4 = (f32[2]{0:T(128)}, f32[2]{0:T(128)}, f32[2]{0:T(128)}, f32[2]{0:T(128)}) fusion(f32[4,1]{1,0:T(4,128)S(1)} %fusion, f32[]{:T(128)} %bitcast.13), kind=kLoop, calls=%fused_computation.10 | loop fusion | bytes 52 | tf_op jit(solution)/shard_map/squeeze | solution.py:114
  22.4 0.0 copy-done
  22.4 3.9 %shard_map.55 = (f32[512,128]{1,0:T(8,128)}, f32[512,1]{1,0:T(8,128)}) custom-call(f32[2]{0:T(128)} %get-tuple-element.17.scalar_ref, bf16[512,128]{1,0:T(8,128)(2,1)} %bitcast.16, bf16[1024,128]{1,0:T(8,128)(2,1)} %copy-done, bf16[512,512]{1,0:T(8,128)(2,1)} %constant.11.clone.upper_ref), custom_call_target="tpu_custom_call" | custom-call | flops 671088640 | bytes 1048576 | tf_op jit(solution)/shard_map/pallas_call | solution.py:91
  26.3 0.0 copy-done.2
  26.3 0.0 copy-done.1
  26.3 4.0 %shard_map.56 = (f32[512,128]{1,0:T(8,128)}, f32[512,1]{1,0:T(8,128)}) custom-call(f32[2]{0:T(128)} %get-tuple-element.19.scalar_ref, bf16[512,128]{1,0:T(8,128)(2,1)} %bitcast.17, bf16[1024,128]{1,0:T(8,128)(2,1)} %copy-done.2, bf16[512,512]{1,0:T(8,128)(2,1)} %constant.11.clone.upper_ref, f32[512,128]{1,0:T(8,128)} %get-tuple-element.11.refs_0_, ...), custom_call_target="tpu_custom_call" | custom-call | flops 671088640 | bytes 1048576 | tf_op jit(solution)/shard_map/pallas_call | solution.py:91
  30.3 4.0 %shard_map.57 = (f32[512,128]{1,0:T(8,128)}, f32[512,1]{1,0:T(8,128)}) custom-call(f32[2]{0:T(128)} %get-tuple-element.18.scalar_ref, bf16[512,128]{1,0:T(8,128)(2,1)} %bitcast.18, bf16[1024,128]{1,0:T(8,128)(2,1)} %copy-done.1, bf16[512,512]{1,0:T(8,128)(2,1)} %constant.11.clone.upper_ref, f32[512,128]{1,0:T(8,128)} %get-tuple-element.13.refs_0_, ...), custom_call_target="tpu_custom_call" | custom-call | flops 671088640 | bytes 1048576 | tf_op jit(solution)/shard_map/pallas_call | solution.py:91
  34.3 0.0 collective-permute-done.2.kv_ref
  34.3 0.0 copy-start.3
  34.3 0.7 %copy-done.3 = bf16[1024,128]{1,0:T(8,128)(2,1)} copy-done((bf16[1024,128]{1,0:T(8,128)(2,1)}, bf16[1024,128]{1,0:T(8,128)(2,1)S(1)}, u32[]{:S(2)}) %copy-start.3) | copy-done | bytes 262168
  35.0 3.9 %shard_map.58 = bf16[512,128]{1,0:T(8,128)(2,1)} custom-call(f32[2]{0:T(128)} %get-tuple-element.20.scalar_ref, bf16[512,128]{1,0:T(8,128)(2,1)} %bitcast.19, bf16[1024,128]{1,0:T(8,128)(2,1)} %copy-done.3, bf16[512,512]{1,0:T(8,128)(2,1)} %constant.11.clone.upper_ref, f32[512,128]{1,0:T(8,128)} %get-tuple-element.15.refs_0_, f32[512,1]{1,0:T(8,128)} %get-tuple-element.16.refs_1_), custom_call_target="tpu_custom_call" | custom-call | flops 671088640 | bytes 1048576 | tf_op jit(solution)/shard_map/pallas_call | solution.py:91
  (1 shorter events, 0.0 us)
Async XLA Ops:
  1.0 21.4 %copy-start = (bf16[1024,128]{1,0:T(8,128)(2,1)}, bf16[1024,128]{1,0:T(8,128)(2,1)S(1)}, u32[]{:S(2)}) copy-start(bf16[1024,128]{1,0:T(8,128)(2,1)S(1)} %pad_maximum_fusion.kv_ref) | copy-start | bytes 786436
  1.0 11.4 %collective-permute-start = (bf16[1024,128]{1,0:T(8,128)(2,1)S(1)}, bf16[1024,128]{1,0:T(8,128)(2,1)S(1)}, u32[]{:S(2)}, u32[]{:S(2)}) collective-permute-start(bf16[1024,128]{1,0:T(8,128)(2,1)S(1)} %pad_maximum_fusion.kv_ref), channel_id=1, source_target_pairs={{0,4},{4,8},{8,12},{12,0},{1,5},{5,9},{9,13},{13,1},{2,6},{6,10},{... | collective-permute-start | bytes 786440 | tf_op jit(solution)/shard_map/ppermute | solution.py:116
  12.4 13.9 %copy-start.2 = (bf16[1024,128]{1,0:T(8,128)(2,1)}, bf16[1024,128]{1,0:T(8,128)(2,1)S(1)}, u32[]{:S(2)}) copy-start(bf16[1024,128]{1,0:T(8,128)(2,1)S(1)} %collective-permute-done.kv_ref) | copy-start | bytes 786436
  12.4 9.3 %collective-permute-start.1 = (bf16[1024,128]{1,0:T(8,128)(2,1)S(1)}, bf16[1024,128]{1,0:T(8,128)(2,1)S(1)}, u32[]{:S(2)}, u32[]{:S(2)}) collective-permute-start(bf16[1024,128]{1,0:T(8,128)(2,1)S(1)} %collective-permute-done.kv_ref), channel_id=1, source_target_pairs={{0,4},{4,8},{8,12},{12,0},{1,5},{5,9},{9,13},{13,1},{2,6},{6,10},{... | collective-permute-start | bytes 786440 | tf_op jit(solution)/shard_map/ppermute | solution.py:116
  21.7 4.6 %copy-start.1 = (bf16[1024,128]{1,0:T(8,128)(2,1)}, bf16[1024,128]{1,0:T(8,128)(2,1)S(1)}, u32[]{:S(2)}) copy-start(bf16[1024,128]{1,0:T(8,128)(2,1)S(1)} %collective-permute-done.1.kv_ref) | copy-start | bytes 786436
  21.7 12.6 %collective-permute-start.2 = (bf16[1024,128]{1,0:T(8,128)(2,1)S(1)}, bf16[1024,128]{1,0:T(8,128)(2,1)S(1)}, u32[]{:S(2)}, u32[]{:S(2)}) collective-permute-start(bf16[1024,128]{1,0:T(8,128)(2,1)S(1)} %collective-permute-done.1.kv_ref), channel_id=1, source_target_pairs={{0,4},{4,8},{8,12},{12,0},{1,5},{5,9},{9,13},{13,1},{2,6},{6,10},{... | collective-permute-start | bytes 786440 | tf_op jit(solution)/shard_map/ppermute | solution.py:116
  34.3 0.7 %copy-start.3 = (bf16[1024,128]{1,0:T(8,128)(2,1)}, bf16[1024,128]{1,0:T(8,128)(2,1)S(1)}, u32[]{:S(2)}) copy-start(bf16[1024,128]{1,0:T(8,128)(2,1)S(1)} %collective-permute-done.2.kv_ref) | copy-start | bytes 786436
where the time goes:
time: 39.2 us; the launch traced here: 39 us
  waiting for transfers between devices  16.9 us (43%)
  Pallas kernels  15.9 us (41%)
  starting transfers between devices  3.11 us (8%)
  local copies, waits for them, and re-layouts  1.37 us (3%)
  other arithmetic  0.99 us (3%)
  between operations  0.69 us (2%)
    ppermute x3, waiting for transfers between devices, one_head(): kv = lax.ppermute(kv, 'ctx', route)  16.9 us
    pallas_call x4, Pallas kernels, pair_terms(): pl.pallas_call(kernel, grid=(rows // tile,), in_specs=in_specs, out_specs...  15.9 us
    ppermute x3, starting transfers between devices, one_head(): kv = lax.ppermute(kv, 'ctx', route)  3.11 us
    concatenate x1, other arithmetic, one_head(): kv = jnp.concatenate([k_own, v_own], axis=0)  0.99 us
  transfers between devices with their start and end apart: 3, of which 2 were waited for; matrix products, arithmetic and copies ran while one was open for 2% of the time, Pallas kernels for 31%

commit v1 on v0

--- a/solution.py
+++ b/solution.py
@@ -11,6 +11,8 @@
 
 
 ROW_TILE = 256
+LOG2E = 1.4426950408889634
+LN2 = 0.6931471805599453
 
 
 def pair_kernel(scalar_ref, q_ref, kv_ref, upper_ref, *refs, diag, scale, last):
@@ -28,12 +30,10 @@
             (((1,), (1,)), ((), ())),
             preferred_element_type=jnp.float32,
         )
-        * scale
-        + scalar_ref[0]
+        * (scale * LOG2E)
+        + scalar_ref[0] * LOG2E
     )
-    soft = jnp.log1p(jnp.exp(-jnp.abs(score)))
-    spent = jnp.maximum(score, 0.0) + soft
-    logsig = jnp.minimum(score, 0.0) - soft
+    spent = jnp.maximum(score, 0.0) + jnp.log2(1.0 + jnp.exp2(-jnp.abs(score)))
     if diag:
         row = pl.program_id(0) * tile + lax.broadcasted_iota(jnp.int32, (tile, keys), 0)
         col = lax.broadcasted_iota(jnp.int32, (tile, keys), 1)
@@ -45,11 +45,11 @@
     later = jnp.dot(high, upper, preferred_element_type=jnp.float32) + jnp.dot(
         low, upper, preferred_element_type=jnp.float32
     )
-    weight = jnp.exp(logsig - later)
+    weight = jnp.exp2((score - spent) - later)
     if diag:
         weight = jnp.where(live, weight, 0.0)
     part = jnp.dot(weight.astype(jnp.bfloat16), kv_ref[keys:, :], preferred_element_type=jnp.float32)
-    tot = later[:, 0:1] + spent[:, 0:1]
+    tot = (later[:, 0:1] + spent[:, 0:1]) * LN2
     if diag:
         summed_ref[...] = part
         spent_ref[...] = tot
@@ -60,6 +60,23 @@
     summed_ref[...] = summed.astype(summed_ref.dtype)
     if not last:
         spent_ref[...] = jnp.where(use, before + tot, before)
+
+
+def stack_kernel(k_ref, v_ref, out_ref):
+    rows = k_ref.shape[0]
+    out_ref[:rows, :] = k_ref[...]
+    out_ref[rows:, :] = v_ref[...]
+
+
+def stacked(k, v):
+    rows, width = k.shape
+    whole = pl.BlockSpec(memory_space=pltpu.VMEM)
+    return pl.pallas_call(
+        stack_kernel,
+        in_specs=[whole, whole],
+        out_specs=whole,
+        out_shape=jax.ShapeDtypeStruct((2 * rows, width), k.dtype),
+    )(k, v)
 
 
 def pair_terms(q, kv, upper, scalars, carried=None, last=False):
@@ -76,7 +93,7 @@
     in_specs = [
         pl.BlockSpec(memory_space=pltpu.SMEM),
         rows_spec,
-        pl.BlockSpec((2 * keys, width), lambda r: (0, 0)),
+        pl.BlockSpec(memory_space=pltpu.VMEM),
         pl.BlockSpec((keys, keys), lambda r: (0, 0)),
     ]
     args = [scalars, q, kv, upper]
@@ -106,7 +123,7 @@
     route = [(i, (i + 1) % count) for i in range(count)]
     keys = k_own.shape[0]
     upper = jnp.asarray(np.triu(np.ones((keys, keys), np.float32), 1).T, jnp.bfloat16)
-    kv = jnp.concatenate([k_own, v_own], axis=0)
+    kv = stacked(k_own, v_own)
     steps = jnp.arange(count, dtype=jnp.int32)
     table = jnp.stack(
         [jnp.broadcast_to(offset, (count,)), jnp.where(place >= steps, 1.0, 0.0)], axis=1

time: 39.2 us -> 39 us (level)
  other arithmetic: 0.99 us -> 0.01 us
  Pallas kernels: 15.9 us -> 16.5 us
    pallas_call x0 -> x1, Pallas kernels: none -> 1.69 us  [stacked(): pl.pallas_call(stack_kernel, in_specs=[whole, whole], out_specs=whole, ou...]
    pallas_call x4, Pallas kernels: 15.9 us -> 14.8 us  [pair_terms(): pl.pallas_call(kernel, grid=(rows // tile,), in_specs=in_specs, out_specs...]
    concatenate x1 -> x0, other arithmetic: 0.99 us -> none  [one_head(): kv = jnp.concatenate([k_own, v_own], axis=0)]
  transfers between devices with their start and end apart: 3 -> 3, of which waited for: 2 -> 2; matrix products, arithmetic and copies ran while one was open for 2% -> 2% of each run, Pallas kernels for 31% -> 29%
where the time goes in v1:
time: 39 us; the launch traced here: 38.7 us
  waiting for transfers between devices  17.1 us (44%)
  Pallas kernels  16.5 us (42%)
  starting transfers between devices  3.06 us (8%)
  local copies, waits for them, and re-layouts  1.36 us (3%)
  between operations  0.68 us (2%)
    ppermute x3, waiting for transfers between devices, one_head(): kv = lax.ppermute(kv, 'ctx', route)  17.1 us
    pallas_call x4, Pallas kernels, pair_terms(): pl.pallas_call(kernel, grid=(rows // tile,), in_specs=in_specs, out_specs...  14.8 us
    ppermute x3, starting transfers between devices, one_head(): kv = lax.ppermute(kv, 'ctx', route)  3.06 us
    pallas_call x1, Pallas kernels, stacked(): pl.pallas_call(stack_kernel, in_specs=[whole, whole], out_specs=whole, ou...  1.69 us
  transfers between devices with their start and end apart: 3, of which 2 were waited for; matrix products, arithmetic and copies ran while one was open for 2% of the time, Pallas kernels for 29%

profile of v1, /device:TPU:0, one launch (start us, length us, event | category | flops | bytes accessed | tf_op | source)
XLA Modules:
  0.0 38.7 jit_solution(5646059644329941240)
XLA Ops:
  0.0 1.7 %shard_map.55.kv_ref = bf16[1024,128]{1,0:T(8,128)(2,1)} custom-call(bf16[512,128]{1,0:T(8,128)(2,1)} %bitcast.14, bf16[512,128]{1,0:T(8,128)(2,1)} %bitcast.15), custom_call_target="tpu_custom_call" | custom-call | tf_op jit(solution)/shard_map/pallas_call | solution.py:74
  1.7 3.1 %collective-permute-start = (bf16[1024,128]{1,0:T(8,128)(2,1)}, bf16[1024,128]{1,0:T(8,128)(2,1)S(1)}, u32[]{:S(2)}, u32[]{:S(2)}) collective-permute-start(bf16[1024,128]{1,0:T(8,128)(2,1)} %shard_map.55.kv_ref), channel_id=1, source_target_pairs={{0,4},{4,8},{8,12},{12,0},{1,5},{5,9},{9,13},{13,1},{2,6},{6,10},{... | collective-permute-start | bytes 786440 | tf_op jit(solution)/shard_map/ppermute | solution.py:133
  4.7 8.5 %collective-permute-done.kv_ref = bf16[1024,128]{1,0:T(8,128)(2,1)S(1)} collective-permute-done((bf16[1024,128]{1,0:T(8,128)(2,1)}, bf16[1024,128]{1,0:T(8,128)(2,1)S(1)}, u32[]{:S(2)}, u32[]{:S(2)}) %collective-permute-start) | collective-permute-done | bytes 262176 | tf_op jit(solution)/shard_map/ppermute | solution.py:133
  13.3 0.0 copy-start.1
  13.3 0.0 collective-permute-start.1
  14.0 8.6 %collective-permute-done.1.kv_ref = bf16[1024,128]{1,0:T(8,128)(2,1)S(1)} collective-permute-done((bf16[1024,128]{1,0:T(8,128)(2,1)S(1)}, bf16[1024,128]{1,0:T(8,128)(2,1)S(1)}, u32[]{:S(2)}, u32[]{:S(2)}) %collective-permute-start.1) | collective-permute-done | bytes 262176 | tf_op jit(solution)/shard_map/ppermute | solution.py:133
  22.6 0.0 copy-start
  22.6 0.0 collective-permute-start.2
  22.6 0.7 %fusion.4 = (f32[2]{0:T(128)}, f32[2]{0:T(128)}, f32[2]{0:T(128)}, f32[2]{0:T(128)}) fusion(f32[4,1]{1,0:T(4,128)S(1)} %fusion, f32[]{:T(128)} %bitcast.13), kind=kLoop, calls=%fused_computation.9 | loop fusion | bytes 52 | tf_op jit(solution)/shard_map/squeeze | solution.py:131
  23.2 3.6 %shard_map.56 = (f32[512,128]{1,0:T(8,128)}, f32[512,1]{1,0:T(8,128)}) custom-call(f32[2]{0:T(128)} %get-tuple-element.17.scalar_ref, bf16[512,128]{1,0:T(8,128)(2,1)} %bitcast.16, bf16[1024,128]{1,0:T(8,128)(2,1)} %shard_map.55.kv_ref, bf16[512,512]{1,0:T(8,128)(2,1)} %constant.11.clone.upper_ref), custom_call_target="tpu_custom_call" | custom-call | flops 671088640 | bytes 1048576 | tf_op jit(solution)/shard_map/pallas_call | solution.py:108
  26.8 0.0 copy-done.1
  26.8 0.0 copy-done
  26.8 3.8 %shard_map.57 = (f32[512,128]{1,0:T(8,128)}, f32[512,1]{1,0:T(8,128)}) custom-call(f32[2]{0:T(128)} %get-tuple-element.19.scalar_ref, bf16[512,128]{1,0:T(8,128)(2,1)} %bitcast.17, bf16[1024,128]{1,0:T(8,128)(2,1)} %copy-done.1, bf16[512,512]{1,0:T(8,128)(2,1)} %constant.11.clone.upper_ref, f32[512,128]{1,0:T(8,128)} %get-tuple-element.11.refs_0_, ...), custom_call_target="tpu_custom_call" | custom-call | flops 671088640 | bytes 1048576 | tf_op jit(solution)/shard_map/pallas_call | solution.py:108
  30.6 3.8 %shard_map.58 = (f32[512,128]{1,0:T(8,128)}, f32[512,1]{1,0:T(8,128)}) custom-call(f32[2]{0:T(128)} %get-tuple-element.18.scalar_ref, bf16[512,128]{1,0:T(8,128)(2,1)} %bitcast.18, bf16[1024,128]{1,0:T(8,128)(2,1)} %copy-done, bf16[512,512]{1,0:T(8,128)(2,1)} %constant.11.clone.upper_ref, f32[512,128]{1,0:T(8,128)} %get-tuple-element.13.refs_0_, ...), custom_call_target="tpu_custom_call" | custom-call | flops 671088640 | bytes 1048576 | tf_op jit(solution)/shard_map/pallas_call | solution.py:108
  34.3 0.0 collective-permute-done.2.kv_ref
  34.4 0.0 copy-start.2
  34.4 0.7 %copy-done.2 = bf16[1024,128]{1,0:T(8,128)(2,1)} copy-done((bf16[1024,128]{1,0:T(8,128)(2,1)}, bf16[1024,128]{1,0:T(8,128)(2,1)S(1)}, u32[]{:S(2)}) %copy-start.2) | copy-done | bytes 262168
  35.1 3.7 %shard_map.59 = bf16[512,128]{1,0:T(8,128)(2,1)} custom-call(f32[2]{0:T(128)} %get-tuple-element.20.scalar_ref, bf16[512,128]{1,0:T(8,128)(2,1)} %bitcast.19, bf16[1024,128]{1,0:T(8,128)(2,1)} %copy-done.2, bf16[512,512]{1,0:T(8,128)(2,1)} %constant.11.clone.upper_ref, f32[512,128]{1,0:T(8,128)} %get-tuple-element.15.refs_0_, f32[512,1]{1,0:T(8,128)} %get-tuple-element.16.refs_1_), custom_call_target="tpu_custom_call" | custom-call | flops 671088640 | bytes 1048576 | tf_op jit(solution)/shard_map/pallas_call | solution.py:108
  (1 shorter events, 0.0 us)
Async XLA Ops:
  1.7 11.6 %collective-permute-start = (bf16[1024,128]{1,0:T(8,128)(2,1)}, bf16[1024,128]{1,0:T(8,128)(2,1)S(1)}, u32[]{:S(2)}, u32[]{:S(2)}) collective-permute-start(bf16[1024,128]{1,0:T(8,128)(2,1)} %shard_map.55.kv_ref), channel_id=1, source_target_pairs={{0,4},{4,8},{8,12},{12,0},{1,5},{5,9},{9,13},{13,1},{2,6},{6,10},{... | collective-permute-start | bytes 786440 | tf_op jit(solution)/shard_map/ppermute | solution.py:133
  13.3 13.5 %copy-start.1 = (bf16[1024,128]{1,0:T(8,128)(2,1)}, bf16[1024,128]{1,0:T(8,128)(2,1)S(1)}, u32[]{:S(2)}) copy-start(bf16[1024,128]{1,0:T(8,128)(2,1)S(1)} %collective-permute-done.kv_ref) | copy-start | bytes 786436
  13.3 9.3 %collective-permute-start.1 = (bf16[1024,128]{1,0:T(8,128)(2,1)S(1)}, bf16[1024,128]{1,0:T(8,128)(2,1)S(1)}, u32[]{:S(2)}, u32[]{:S(2)}) collective-permute-start(bf16[1024,128]{1,0:T(8,128)(2,1)S(1)} %collective-permute-done.kv_ref), channel_id=1, source_target_pairs={{0,4},{4,8},{8,12},{12,0},{1,5},{5,9},{9,13},{13,1},{2,6},{6,10},{... | collective-permute-start | bytes 786440 | tf_op jit(solution)/shard_map/ppermute | solution.py:133
  22.6 4.3 %copy-start = (bf16[1024,128]{1,0:T(8,128)(2,1)}, bf16[1024,128]{1,0:T(8,128)(2,1)S(1)}, u32[]{:S(2)}) copy-start(bf16[1024,128]{1,0:T(8,128)(2,1)S(1)} %collective-permute-done.1.kv_ref) | copy-start | bytes 786436
  22.6 11.8 %collective-permute-start.2 = (bf16[1024,128]{1,0:T(8,128)(2,1)S(1)}, bf16[1024,128]{1,0:T(8,128)(2,1)S(1)}, u32[]{:S(2)}, u32[]{:S(2)}) collective-permute-start(bf16[1024,128]{1,0:T(8,128)(2,1)S(1)} %collective-permute-done.1.kv_ref), channel_id=1, source_target_pairs={{0,4},{4,8},{8,12},{12,0},{1,5},{5,9},{9,13},{13,1},{2,6},{6,10},{... | collective-permute-start | bytes 786440 | tf_op jit(solution)/shard_map/ppermute | solution.py:133
  34.4 0.7 %copy-start.2 = (bf16[1024,128]{1,0:T(8,128)(2,1)}, bf16[1024,128]{1,0:T(8,128)(2,1)S(1)}, u32[]{:S(2)}) copy-start(bf16[1024,128]{1,0:T(8,128)(2,1)S(1)} %collective-permute-done.2.kv_ref) | copy-start | bytes 786436
